TPU v7x, 256 devices: a whole 4x4x8 slice. The times are simulated.
256 devices in a mesh: seq: 32 (over x_hi, z, core), tp: 8 (over y, x_lo).
Axes of the slice: x: 4 (x_hi: 2, x_lo: 2; x = x_hi * 2 + x_lo), y: 4, z: 8, core: 2. Of those that a mesh axis runs over, the one named last changes fastest.
Arguments:
- proj: bfloat16 [4096, 3, 8192], P('seq', None, 'tp'), may hold values from -6 to 6
- cotangent: bfloat16 [4096, 8192], P('seq', 'tp'), may hold values from -6 to 6
- out_weight: bfloat16 [8192, 8192], P('seq', 'tp'), may hold values from -0.125 to 0.125
- short_weight: float32 [7, 3, 8192], P(None, None, 'tp'), may hold values from -2 to 2
- long_filter: float32 [4096, 8192], P('seq', 'tp')
Outputs:
- grad_proj: bfloat16 [4096, 3, 8192], P('seq', None, 'tp')
- grad_short: float32 [7, 3, 8192], P(None, None, 'tp')
- grad_filter: float32 [4096, 8192], P('seq', 'tp')
All inputs are finite; a program needn't handle non-finite values.
Results may differ from a plain program's by a relative error of at most 0.025.
Values may be sent and summed in bfloat16 or wider, within the bound.
No kernel may reach another device: no remote copies, remote signals or barrier semaphores. Data moves between devices by JAX's collectives and lax.ppermute only.
A program may use at most 128 MiB of HBM per device.

v0:
```python
import math
import jax
import jax.numpy as jnp
from jax import lax
from jax.sharding import PartitionSpec as P

highest = lax.Precision.HIGHEST


def shifted(value, axis, by):
    devices = lax.axis_size(axis)
    pairs = [(i, i + by) for i in range(devices) if 0 <= i + by < devices]
    return lax.ppermute(value, axis, pairs)


def angle_tables(row_count, col_count, modulus):
    row_index = jnp.arange(row_count, dtype=jnp.int32)[:, None]
    col_index = jnp.arange(col_count, dtype=jnp.int32)[None, :]
    phase = (row_index * col_index % modulus).astype(jnp.float32) * (2.0 * math.pi / modulus)
    return (jnp.cos(phase), jnp.sin(phase))


def split_length(length):
    whole_len = 2 * length
    ceiling = 1 << whole_len.bit_length() // 2 - 1
    first_len = 2 * math.gcd(length, ceiling)
    return (first_len, whole_len // first_len)


def spectrum(columns):
    length, channels = columns.shape
    first_len, second_len = split_length(length)
    lower_half = first_len // 2
    whole_len = first_len * second_len
    values = columns.astype(jnp.float32).reshape(lower_half, second_len * channels)
    cos_first, sin_first = angle_tables(first_len, lower_half, first_len)
    real_one = jnp.dot(cos_first, values, precision=highest).reshape(
        first_len, second_len, channels
    )
    imag_one = -jnp.dot(sin_first, values, precision=highest).reshape(
        first_len, second_len, channels
    )
    twist_cos, twist_sin = angle_tables(first_len, second_len, whole_len)
    twist_cos = twist_cos[:, :, None]
    twist_sin = twist_sin[:, :, None]
    real_two = real_one * twist_cos + imag_one * twist_sin
    imag_two = imag_one * twist_cos - real_one * twist_sin
    cos_second, sin_second = angle_tables(second_len, second_len, second_len)
    real_out = jnp.einsum("amc,ml->alc", real_two, cos_second, precision=highest) + jnp.einsum(
        "amc,ml->alc", imag_two, sin_second, precision=highest
    )
    imag_out = jnp.einsum("amc,ml->alc", imag_two, cos_second, precision=highest) - jnp.einsum(
        "amc,ml->alc", real_two, sin_second, precision=highest
    )
    return (real_out, imag_out)


def signal(real_in, imag_in):
    first_len, second_len, channels = real_in.shape
    lower_half = first_len // 2
    whole_len = first_len * second_len
    cos_second, sin_second = angle_tables(second_len, second_len, second_len)
    real_one = jnp.einsum("alc,lm->amc", real_in, cos_second, precision=highest) - jnp.einsum(
        "alc,lm->amc", imag_in, sin_second, precision=highest
    )
    imag_one = jnp.einsum("alc,lm->amc", real_in, sin_second, precision=highest) + jnp.einsum(
        "alc,lm->amc", imag_in, cos_second, precision=highest
    )
    twist_cos, twist_sin = angle_tables(first_len, second_len, whole_len)
    twist_cos = twist_cos[:, :, None]
    twist_sin = twist_sin[:, :, None]
    real_two = real_one * twist_cos - imag_one * twist_sin
    imag_two = real_one * twist_sin + imag_one * twist_cos
    cos_first, sin_first = angle_tables(lower_half, first_len, first_len)
    merged = jnp.dot(
        cos_first, real_two.reshape(first_len, second_len * channels), precision=highest
    ) - jnp.dot(sin_first, imag_two.reshape(first_len, second_len * channels), precision=highest)
    return merged.reshape(lower_half * second_len, channels) / whole_len


def complex_product(left_real, left_imag, right_real, right_imag):
    return (
        left_real * right_real - left_imag * right_imag,
        left_real * right_imag + left_imag * right_real,
    )


def conj_product(left_real, left_imag, right_real, right_imag):
    return (
        left_real * right_real + left_imag * right_imag,
        left_imag * right_real - left_real * right_imag,
    )


def times_bf16(left_array, right_array):
    return (left_array.astype(jnp.float32) * right_array.astype(jnp.float32)).astype(jnp.bfloat16)


def body(proj, cotangent, out_weight, short_weight, long_filter):
    tok_rows = proj.shape[0]
    channels = proj.shape[2]
    taps_count = short_weight.shape[0]
    rim_rows = taps_count - 1
    partial_value = lax.dot_general(
        cotangent,
        lax.all_gather(out_weight, "seq", axis=0, tiled=True),
        (((1,), (1,)), ((), ())),
        preferred_element_type=jnp.float32,
    )
    grad_out = lax.psum_scatter(
        partial_value.astype(jnp.bfloat16), "tp", scatter_dimension=1, tiled=True
    )
    lower_rows = shifted(proj[tok_rows - rim_rows :], "seq", 1)
    extended = jnp.concatenate([lower_rows, proj], axis=0)
    primed = short_weight[0] * extended[rim_rows : rim_rows + tok_rows]
    for offset in range(1, taps_count):
        primed = (
            primed
            + short_weight[offset] * extended[rim_rows - offset : rim_rows - offset + tok_rows]
        )
    primed = primed.astype(jnp.bfloat16)
    query_conv = primed[:, 0]
    keys_conv = primed[:, 1]
    value_conv = primed[:, 2]
    gated_input = times_bf16(keys_conv, value_conv)
    filter_cols = lax.all_to_all(
        long_filter.astype(jnp.bfloat16), "seq", split_axis=1, concat_axis=0, tiled=True
    ).astype(long_filter.dtype)
    filter_real, filter_imag = spectrum(filter_cols)
    gated_cols = lax.all_to_all(gated_input, "seq", split_axis=1, concat_axis=0, tiled=True)
    gated_real, gated_imag = spectrum(gated_cols)
    conv_cols = signal(*complex_product(gated_real, gated_imag, filter_real, filter_imag)).astype(
        jnp.bfloat16
    )
    conv_out = lax.all_to_all(conv_cols, "seq", split_axis=0, concat_axis=1, tiled=True)
    grad_query = times_bf16(grad_out, conv_out)
    grad_conv = times_bf16(grad_out, query_conv)
    grad_cols = lax.all_to_all(grad_conv, "seq", split_axis=1, concat_axis=0, tiled=True)
    grad_real, grad_imag = spectrum(grad_cols)
    gated_grad_cols = signal(*conj_product(grad_real, grad_imag, filter_real, filter_imag)).astype(
        jnp.bfloat16
    )
    filter_grad_cols = signal(*conj_product(grad_real, grad_imag, gated_real, gated_imag))
    gated_grad = lax.all_to_all(gated_grad_cols, "seq", split_axis=0, concat_axis=1, tiled=True)
    grad_filter = lax.all_to_all(
        filter_grad_cols.astype(jnp.bfloat16), "seq", split_axis=0, concat_axis=1, tiled=True
    ).astype(filter_grad_cols.dtype)
    grad_keys = times_bf16(gated_grad, value_conv)
    grad_value = times_bf16(gated_grad, keys_conv)
    grad_primed = jnp.stack([grad_query, grad_keys, grad_value], axis=1)
    next_rows = shifted(grad_primed[:rim_rows], "seq", -1)
    trailing = jnp.concatenate([grad_primed, next_rows], axis=0)
    grad_sum = short_weight[0] * trailing[0:tok_rows]
    for offset in range(1, taps_count):
        grad_sum = grad_sum + short_weight[offset] * trailing[offset : offset + tok_rows]
    grad_proj = grad_sum.astype(jnp.bfloat16)
    grad_wide = grad_primed.astype(jnp.float32)
    local_short = jnp.stack(
        [
            jnp.sum(
                grad_wide
                * extended[rim_rows - offset : rim_rows - offset + tok_rows].astype(jnp.float32),
                axis=0,
            )
            for offset in range(taps_count)
        ]
    )
    short_shape = local_short.shape
    grad_short = lax.psum(local_short.reshape(-1, channels), "seq").reshape(short_shape)
    return (grad_proj, grad_short, grad_filter)


def solution(mesh):
    in_specs = (
        P("seq", None, "tp"),
        P("seq", "tp"),
        P("seq", "tp"),
        P(None, None, "tp"),
        P("seq", "tp"),
    )
    out_specs = (P("seq", None, "tp"), P(None, None, "tp"), P("seq", "tp"))
    return jax.shard_map(body, mesh=mesh, in_specs=in_specs, out_specs=out_specs, check_vma=False)
```

profile of v0, /device:TPU:2, one launch (start us, length us, event | category | flops | bytes accessed | tf_op | source)
XLA Modules:
  0.0 583.1 jit_solution(17212374280899392005)
XLA Ops:
  10.5 1.9 copy.45
  12.4 11.3 %all-to-all-start.1 = ((bf16[128,32,32]{0,2,1:T(8,128)(2,1)}), bf16[128,32,32]{0,2,1:T(8,128)(2,1)S(1)}, u32[]{:S(2)}, u32[]{:S(2)}) async-start(bf16[128,32,32]{0,2,1:T(8,128)(2,1)} %bitcast.8), calls=%async_computation.2 | async-start | bytes 524288 | tf_op jit(solution)/shard_map/all_to_all | solution.py:126
  23.9 128.3 %all-gather.2.cloned.1.call-done = bf16[8192,1024]{1,0:T(8,128)(2,1)} async-done(((bf16[256,1024]{1,0:T(8,128)(2,1)}), bf16[8192,1024]{1,0:T(8,128)(2,1)}) %all-gather.2.cloned.1.call-update) | async-done | bytes 16777232 | tf_op jit(solution)/shard_map/all_gather | solution.py:106
  152.2 12.7 %convolution_convert_fusion = bf16[128,8192]{1,0:T(8,128)(2,1)} fusion(bf16[128,1024]{1,0:T(8,128)(2,1)S(1)} %copy-done, bf16[8192,1024]{1,0:T(8,128)(2,1)} %all-gather.2.cloned.1.call-done), kind=kOutput, calls=%fused_computation | convolution fusion | flops 2148532224 | bytes 19136512 | tf_op jit(solution)/shard_map/dot_general | solution.py:104
  168.5 5.8 all-to-all-start
  178.8 2.1 convolution_subtract_fusion.7
  182.1 2.2 convolution_add_fusion.4
  184.3 4.6 all-to-all-done
  193.8 2.2 convolution_subtract_fusion.8
  196.0 22.9 %reduce-scatter.2.cloned.1.call-done = bf16[128,1024]{1,0:T(8,128)(2,1)} async-done(((bf16[128,8192]{1,0:T(8,128)(2,1)}), bf16[128,1024]{1,0:T(8,128)(2,1)}) %reduce-scatter.2.cloned.1.call-update) | async-done | bytes 262160 | tf_op jit(solution)/shard_map/reduce_scatter | solution.py:110
  220.8 9.2 %all-to-all-start.3 = ((bf16[128,32,32]{0,2,1:T(8,128)(2,1)}), bf16[128,32,32]{0,2,1:T(8,128)(2,1)S(1)}, u32[]{:S(2)}, u32[]{:S(2)}) async-start(bf16[128,32,32]{0,2,1:T(8,128)(2,1)} %bitcast.22), calls=%async_computation.4 | async-start | bytes 524288 | tf_op jit(solution)/shard_map/all_to_all | solution.py:138
  231.1 2.1 convolution_add_fusion.5
  233.3 11.4 %all-to-all-done.3 = bf16[128,32,32]{0,2,1:T(8,128)(2,1)S(1)} async-done(((bf16[128,32,32]{0,2,1:T(8,128)(2,1)}), bf16[128,32,32]{0,2,1:T(8,128)(2,1)S(1)}, u32[]{:S(2)}, u32[]{:S(2)}) %all-to-all-start.3) | async-done | bytes 262176 | tf_op jit(solution)/shard_map/all_to_all | solution.py:138
  252.5 2.0 multiply_subtract_fusion.1
  267.6 3.5 multiply_add_fusion
  279.1 4.0 all-to-all-start.2
  290.1 7.6 %all-to-all-done.2 = bf16[32,128,32]{1,2,0:T(8,128)(2,1)S(1)} async-done(((bf16[32,128,32]{1,2,0:T(8,128)(2,1)}), bf16[32,128,32]{1,2,0:T(8,128)(2,1)S(1)}, u32[]{:S(2)}, u32[]{:S(2)}) %all-to-all-start.2) | async-done | bytes 262176 | tf_op jit(solution)/shard_map/all_to_all | solution.py:135
  297.8 4.1 all-to-all-start.4
  301.9 2.6 fusion.168
  307.9 8.4 %all-to-all-done.4 = bf16[32,128,32]{1,2,0:T(8,128)(2,1)S(1)} async-done(((bf16[32,128,32]{1,2,0:T(8,128)(2,1)}), bf16[32,128,32]{1,2,0:T(8,128)(2,1)S(1)}, u32[]{:S(2)}, u32[]{:S(2)}) %all-to-all-start.4) | async-done | bytes 262176 | tf_op jit(solution)/shard_map/all_to_all | solution.py:144
  316.3 3.9 all-to-all-start.5
  325.4 9.4 %all-to-all-done.5 = bf16[32,128,32]{1,2,0:T(8,128)(2,1)S(1)} async-done(((bf16[32,128,32]{1,2,0:T(8,128)(2,1)}), bf16[32,128,32]{1,2,0:T(8,128)(2,1)S(1)}, u32[]{:S(2)}, u32[]{:S(2)}) %all-to-all-start.5) | async-done | bytes 262176 | tf_op jit(solution)/shard_map/all_to_all | solution.py:145
  336.1 2.3 fusion.19
  338.4 236.1 %all-reduce.2.cloned.1.call-done = f32[7,3,1024]{2,1,0:T(4,128)} async-done(((f32[7,3,1024]{2,1,0:T(4,128)}), f32[7,3,1024]{2,1,0:T(4,128)}) %all-reduce.2.cloned.1.call-update) | async-done | bytes 86032 | tf_op jit(solution)/shard_map/psum | solution.py:169
  (137 shorter events, 67.6 us)
Async XLA Ops:
  7.2 145.0 %copy-start = (bf16[128,1024]{1,0:T(8,128)(2,1)S(1)}, bf16[128,1024]{1,0:T(8,128)(2,1)}, u32[]{:S(2)}) copy-start(bf16[128,1024]{1,0:T(8,128)(2,1)} %param.6) | copy-start | bytes 786436
  7.2 16.6 %copy-start.21 = (f32[7,3,1024]{2,0,1:T(8,128)S(1)}, f32[7,3,1024]{2,0,1:T(8,128)}, u32[]{:S(2)}) copy-start(f32[7,3,1024]{2,0,1:T(8,128)} %param.8) | copy-start | bytes 258052
  7.2 145.0 %all-gather.2.cloned.1.call-start = ((), (), s32[]{:S(2)}) async-start(), calls=%async_computation.7 | async-start | bytes 17301504 | tf_op jit(solution)/shard_map/all_gather | solution.py:106
  8.7 156.4 %collective-permute-start = (bf16[6,3,1024]{2,0,1:T(8,128)(2,1)S(1)}, bf16[6,3,1024]{2,0,1:T(8,128)(2,1)S(1)}, u32[]{:S(2)}, u32[]{:S(2)}) collective-permute-start(bf16[6,3,1024]{2,0,1:T(8,128)(2,1)S(1)} %slice.87), channel_id=1, source_target_pairs={{0,8},{8,16},{16,24},{24,32},{32,40},{40,48},{48,56},{56,64},{64,7... | collective-permute-start | bytes 110600 | tf_op jit(solution)/shard_map/ppermute | solution.py:13
  12.4 156.1 %all-to-all-start.1 = ((bf16[128,32,32]{0,2,1:T(8,128)(2,1)}), bf16[128,32,32]{0,2,1:T(8,128)(2,1)S(1)}, u32[]{:S(2)}, u32[]{:S(2)}) async-start(bf16[128,32,32]{0,2,1:T(8,128)(2,1)} %bitcast.8), calls=%async_computation.2 | async-start | bytes 524288 | tf_op jit(solution)/shard_map/all_to_all | solution.py:126
  23.7 195.2 %reduce-scatter.2.cloned.1.call-start = ((), (), s32[]{:S(2)}) async-start(), calls=%async_computation.8 | async-start | bytes 2359296 | tf_op jit(solution)/shard_map/reduce_scatter | solution.py:110
  165.0 3.5 copy-start.11
  165.0 3.5 copy-start.13
  165.0 3.5 copy-start.15
  165.0 3.5 copy-start.17
  165.2 3.3 copy-start.19
  168.5 20.3 %all-to-all-start = ((bf16[128,32,32]{0,2,1:T(8,128)(2,1)}), bf16[128,32,32]{0,2,1:T(8,128)(2,1)S(1)}, u32[]{:S(2)}, u32[]{:S(2)}) async-start(bf16[128,32,32]{0,2,1:T(8,128)(2,1)} %bitcast.2), calls=%async_computation.1 | async-start | bytes 524288 | tf_op jit(solution)/shard_map/all_to_all | solution.py:130
  220.8 23.9 %all-to-all-start.3 = ((bf16[128,32,32]{0,2,1:T(8,128)(2,1)}), bf16[128,32,32]{0,2,1:T(8,128)(2,1)S(1)}, u32[]{:S(2)}, u32[]{:S(2)}) async-start(bf16[128,32,32]{0,2,1:T(8,128)(2,1)} %bitcast.22), calls=%async_computation.4 | async-start | bytes 524288 | tf_op jit(solution)/shard_map/all_to_all | solution.py:138
  250.4 1.5 copy-start.3
  250.4 1.8 copy-start.4
  250.4 2.1 copy-start.5
  279.1 5.9 %copy-start.6 = (f32[128,64,32]{0,1,2:T(8,128)S(1)}, f32[128,64,32]{0,1,2:T(8,128)}, u32[]{:S(2)}) copy-start(f32[128,64,32]{0,1,2:T(8,128)} %get-tuple-element.48) | copy-start | bytes 3145732
  279.1 18.7 %all-to-all-start.2 = ((bf16[32,128,32]{1,2,0:T(8,128)(2,1)}), bf16[32,128,32]{1,2,0:T(8,128)(2,1)S(1)}, u32[]{:S(2)}, u32[]{:S(2)}) async-start(bf16[32,128,32]{1,2,0:T(8,128)(2,1)} %copy.52), calls=%async_computation.3 | async-start | bytes 524288 | tf_op jit(solution)/shard_map/all_to_all | solution.py:135
  297.8 18.5 %all-to-all-start.4 = ((bf16[32,128,32]{1,2,0:T(8,128)(2,1)}), bf16[32,128,32]{1,2,0:T(8,128)(2,1)S(1)}, u32[]{:S(2)}, u32[]{:S(2)}) async-start(bf16[32,128,32]{1,2,0:T(8,128)(2,1)} %copy.61), calls=%async_computation.5 | async-start | bytes 524288 | tf_op jit(solution)/shard_map/all_to_all | solution.py:144
  316.3 18.5 %all-to-all-start.5 = ((bf16[32,128,32]{1,2,0:T(8,128)(2,1)}), bf16[32,128,32]{1,2,0:T(8,128)(2,1)S(1)}, u32[]{:S(2)}, u32[]{:S(2)}) async-start(bf16[32,128,32]{1,2,0:T(8,128)(2,1)} %copy.66), calls=%async_computation.6 | async-start | bytes 524288 | tf_op jit(solution)/shard_map/all_to_all | solution.py:145
  320.2 254.4 %all-reduce.2.cloned.1.call-start = ((), (), s32[]{:S(2)}) async-start(), calls=%async_computation.9 | async-start | bytes 229376 | tf_op jit(solution)/shard_map/psum | solution.py:169
  324.0 11.9 %collective-permute-start.1 = (bf16[6,3,1024]{2,0,1:T(8,128)(2,1)S(1)}, bf16[6,3,1024]{2,0,1:T(8,128)(2,1)S(1)}, u32[]{:S(2)}, u32[]{:S(2)}) collective-permute-start(bf16[6,3,1024]{2,0,1:T(8,128)(2,1)S(1)} %slice.122), channel_id=1, source_target_pairs={{8,0},{16,8},{24,16},{32,24},{40,32},{48,40},{56,48},{64,56},{72,6... | collective-permute-start | bytes 110600 | tf_op jit(solution)/shard_map/ppermute | solution.py:13
  325.4 10.5 %copy-start.10 = (f32[7,3,1024]{2,1,0:T(4,128)}, f32[7,3,1024]{2,1,0:T(4,128)S(1)}, u32[]{:S(2)}) copy-start(f32[7,3,1024]{2,1,0:T(4,128)S(1)} %constant_dynamic-update-slice_fusion) | copy-start | bytes 258052
  336.1 240.0 %copy-start.1 = (bf16[128,1024]{1,0:T(8,128)(2,1)S(1)}, bf16[128,1024]{1,0:T(8,128)(2,1)}, u32[]{:S(2)}) copy-start(bf16[128,1024]{1,0:T(8,128)(2,1)} %param.6) | copy-start | bytes 786436
  (9 other events, 10.3 us)
Sparse Core Ops, SparseCore 0:
  10.8 141.3 all-gather.1
  165.1 53.7 reduce-scatter.1
  336.1 238.4 all-reduce.1
where the time goes:
time: 589 us; the launch traced here: 583 us
  waiting for transfers between devices  429 us (73%)
  matrix products  62.1 us (11%)
  starting transfers between devices  41.5 us (7%)
  local copies, waits for them, and re-layouts  27.9 us (5%)
  between operations  15 us (3%)
  other arithmetic  7.24 us (1%)
    psum x1, waiting for transfers between devices, body(): lax.psum(local_short.reshape(-1, channels), 'seq').reshape(short_shape)  236 us
    all_gather x1, waiting for transfers between devices, body(): lax.all_gather(out_weight, 'seq', axis=0, tiled=True)  128 us
    reduce_scatter x1, waiting for transfers between devices, body(): lax.psum_scatter(partial_value.astype(jnp.bfloat16), 'tp', scatter_dimens...  22.9 us
    dot_general x1, matrix products, body(): lax.dot_general(cotangent, lax.all_gather(out_weight, 'seq', axis=0, tile...  12.7 us
  transfers between devices with their start and end apart: 11, of which 8 were waited for; matrix products, arithmetic and copies ran while one was open for 10% of the time, Pallas kernels for 0%

commit v1 on v0

--- a/solution.py
+++ b/solution.py
@@ -101,9 +101,21 @@
     channels = proj.shape[2]
     taps_count = short_weight.shape[0]
     rim_rows = taps_count - 1
+
+    def attach_outputs_all(here_x, which_axis):
+        return jnp.concatenate(
+            lax.all_to_all(
+                jnp.stack([here_x for _ in range(lax.axis_size(which_axis))], axis=0),
+                which_axis,
+                0,
+                0,
+            ),
+            axis=0,
+        )
+
     partial_value = lax.dot_general(
         cotangent,
-        lax.all_gather(out_weight, "seq", axis=0, tiled=True),
+        attach_outputs_all(out_weight, "seq"),
         (((1,), (1,)), ((), ())),
         preferred_element_type=jnp.float32,
     )

time: 589 us -> 847 us (1.44)
  waiting for transfers between devices: 429 us -> 669 us
  starting transfers between devices: 41.5 us -> 54.5 us
    all_to_all x0 -> x1, waiting for transfers between devices: none -> 368 us  [attach_outputs_all(): lax.all_to_all(jnp.stack([here_x for _ in range(lax.axis_size(which_axis)...]
    all_gather x1 -> x0, waiting for transfers between devices: 128 us -> none  [body(): lax.all_gather(out_weight, 'seq', axis=0, tiled=True)]
    all_to_all x0 -> x1, starting transfers between devices: none -> 10.7 us  [attach_outputs_all(): lax.all_to_all(jnp.stack([here_x for _ in range(lax.axis_size(which_axis)...]
  transfers between devices with their start and end apart: 11 -> 11, of which waited for: 8 -> 8; matrix products, arithmetic and copies ran while one was open for 10% -> 7% of each run, Pallas kernels for 0% -> 0%
where the time goes in v1:
time: 847 us; the launch traced here: 840 us
  waiting for transfers between devices  669 us (79%)
  matrix products  62.1 us (7%)
  starting transfers between devices  54.5 us (6%)
  local copies, waits for them, and re-layouts  32 us (4%)
  between operations  15.3 us (2%)
    all_to_all x1, waiting for transfers between devices, attach_outputs_all(): lax.all_to_all(jnp.stack([here_x for _ in range(lax.axis_size(which_axis)...  368 us
    psum x1, waiting for transfers between devices, body(): lax.psum(local_short.reshape(-1, channels), 'seq').reshape(short_shape)  236 us
    reduce_scatter x1, waiting for transfers between devices, body(): lax.psum_scatter(partial_value.astype(jnp.bfloat16), 'tp', scatter_dimens...  24.2 us
  transfers between devices with their start and end apart: 11, of which 8 were waited for; matrix products, arithmetic and copies ran while one was open for 7% of the time, Pallas kernels for 0%

profile of v1, /device:TPU:2, one launch (start us, length us, event | category | flops | bytes accessed | tf_op | source)
XLA Modules:
  0.0 840.5 jit_solution(10240156548089646198)
XLA Ops:
  7.2 6.8 stack.22
  14.0 10.7 %all-to-all-start = ((bf16[32,256,1024]{2,1,0:T(8,128)(2,1)}), bf16[32,256,1024]{2,1,0:T(8,128)(2,1)}, u32[]{:S(2)}, u32[]{:S(2)}) async-start(bf16[32,256,1024]{2,1,0:T(8,128)(2,1)} %stack.22), calls=%async_computation | async-start | bytes 33554432 | tf_op jit(solution)/shard_map/all_to_all | solution.py:107
  27.8 367.6 %all-to-all-done = bf16[32,256,1024]{2,1,0:T(8,128)(2,1)} async-done(((bf16[32,256,1024]{2,1,0:T(8,128)(2,1)}), bf16[32,256,1024]{2,1,0:T(8,128)(2,1)}, u32[]{:S(2)}, u32[]{:S(2)}) %all-to-all-start) | async-done | bytes 16777248 | tf_op jit(solution)/shard_map/all_to_all | solution.py:107
  395.4 9.1 %all-to-all-start.2 = ((bf16[128,32,32]{0,2,1:T(8,128)(2,1)}), bf16[128,32,32]{0,2,1:T(8,128)(2,1)S(1)}, u32[]{:S(2)}, u32[]{:S(2)}) async-start(bf16[128,32,32]{0,2,1:T(8,128)(2,1)} %bitcast.9), calls=%async_computation.3 | async-start | bytes 524288 | tf_op jit(solution)/shard_map/all_to_all | solution.py:138
  404.5 12.7 %convolution_convert_fusion = bf16[128,8192]{1,0:T(8,128)(2,1)} fusion(bf16[128,1024]{1,0:T(8,128)(2,1)S(1)} %copy-done, bf16[8192,1024]{1,0:T(8,128)(2,1)} %bitcast), kind=kOutput, calls=%fused_computation | convolution fusion | flops 2148532224 | bytes 19136512 | tf_op jit(solution)/shard_map/dot_general | solution.py:116
  420.0 10.0 %all-to-all-start.1 = ((bf16[128,32,32]{0,2,1:T(8,128)(2,1)}), bf16[128,32,32]{0,2,1:T(8,128)(2,1)S(1)}, u32[]{:S(2)}, u32[]{:S(2)}) async-start(bf16[128,32,32]{0,2,1:T(8,128)(2,1)} %bitcast.3), calls=%async_computation.2 | async-start | bytes 524288 | tf_op jit(solution)/shard_map/all_to_all | solution.py:142
  434.6 2.2 convolution_add_fusion.4
  437.9 2.1 convolution_subtract_fusion.7
  440.0 4.6 all-to-all-done.1
  449.6 2.2 convolution_add_fusion.5
  451.8 24.2 %reduce-scatter.2.cloned.1.call-done = bf16[128,1024]{1,0:T(8,128)(2,1)} async-done(((bf16[128,8192]{1,0:T(8,128)(2,1)}), bf16[128,1024]{1,0:T(8,128)(2,1)}) %reduce-scatter.2.cloned.1.call-update) | async-done | bytes 262160 | tf_op jit(solution)/shard_map/reduce_scatter | solution.py:122
  477.8 9.2 %all-to-all-start.4 = ((bf16[128,32,32]{0,2,1:T(8,128)(2,1)}), bf16[128,32,32]{0,2,1:T(8,128)(2,1)S(1)}, u32[]{:S(2)}, u32[]{:S(2)}) async-start(bf16[128,32,32]{0,2,1:T(8,128)(2,1)} %bitcast.23), calls=%async_computation.5 | async-start | bytes 524288 | tf_op jit(solution)/shard_map/all_to_all | solution.py:150
  488.2 2.1 convolution_subtract_fusion.8
  490.3 11.3 %all-to-all-done.4 = bf16[128,32,32]{0,2,1:T(8,128)(2,1)S(1)} async-done(((bf16[128,32,32]{0,2,1:T(8,128)(2,1)}), bf16[128,32,32]{0,2,1:T(8,128)(2,1)S(1)}, u32[]{:S(2)}, u32[]{:S(2)}) %all-to-all-start.4) | async-done | bytes 262176 | tf_op jit(solution)/shard_map/all_to_all | solution.py:150
  524.6 3.5 multiply_add_fusion
  536.1 4.0 all-to-all-start.3
  547.2 7.6 all-to-all-done.3
  554.8 4.1 all-to-all-start.5
  558.9 2.6 fusion.168
  565.0 8.4 all-to-all-done.5
  573.3 3.9 all-to-all-start.6
  582.5 9.4 %all-to-all-done.6 = bf16[32,128,32]{1,2,0:T(8,128)(2,1)S(1)} async-done(((bf16[32,128,32]{1,2,0:T(8,128)(2,1)}), bf16[32,128,32]{1,2,0:T(8,128)(2,1)S(1)}, u32[]{:S(2)}, u32[]{:S(2)}) %all-to-all-start.6) | async-done | bytes 262176 | tf_op jit(solution)/shard_map/all_to_all | solution.py:157
  593.1 2.3 fusion.19
  595.4 236.2 %all-reduce.2.cloned.1.call-done = f32[7,3,1024]{2,1,0:T(4,128)} async-done(((f32[7,3,1024]{2,1,0:T(4,128)}), f32[7,3,1024]{2,1,0:T(4,128)}) %all-reduce.2.cloned.1.call-update) | async-done | bytes 86032 | tf_op jit(solution)/shard_map/psum | solution.py:181
  (139 shorter events, 68.5 us)
Async XLA Ops:
  7.2 397.3 %copy-start = (bf16[128,1024]{1,0:T(8,128)(2,1)S(1)}, bf16[128,1024]{1,0:T(8,128)(2,1)}, u32[]{:S(2)}) copy-start(bf16[128,1024]{1,0:T(8,128)(2,1)} %param.6) | copy-start | bytes 786436
  14.0 10.7 %copy-start.7 = (bf16[128,3,1024]{2,0,1:T(8,128)(2,1)S(1)}, bf16[128,3,1024]{2,0,1:T(8,128)(2,1)}, u32[]{:S(2)}) copy-start(bf16[128,3,1024]{2,0,1:T(8,128)(2,1)} %param.5) | copy-start | bytes 2359300
  14.0 12.9 %copy-start.10 = (f32[128,1024]{1,0:T(8,128)S(1)}, f32[128,1024]{1,0:T(8,128)}, u32[]{:S(2)}) copy-start(f32[128,1024]{1,0:T(8,128)} %param.9) | copy-start | bytes 1572868
  14.0 13.7 %copy-start.22 = (f32[7,3,1024]{2,0,1:T(8,128)S(1)}, f32[7,3,1024]{2,0,1:T(8,128)}, u32[]{:S(2)}) copy-start(f32[7,3,1024]{2,0,1:T(8,128)} %param.8) | copy-start | bytes 258052
  14.0 381.3 %all-to-all-start = ((bf16[32,256,1024]{2,1,0:T(8,128)(2,1)}), bf16[32,256,1024]{2,1,0:T(8,128)(2,1)}, u32[]{:S(2)}, u32[]{:S(2)}) async-start(bf16[32,256,1024]{2,1,0:T(8,128)(2,1)} %stack.22), calls=%async_computation | async-start | bytes 33554432 | tf_op jit(solution)/shard_map/all_to_all | solution.py:107
  24.7 392.8 %collective-permute-start = (bf16[6,3,1024]{2,0,1:T(8,128)(2,1)S(1)}, bf16[6,3,1024]{2,0,1:T(8,128)(2,1)S(1)}, u32[]{:S(2)}, u32[]{:S(2)}) collective-permute-start(bf16[6,3,1024]{2,0,1:T(8,128)(2,1)S(1)} %slice.87), channel_id=1, source_target_pairs={{0,8},{8,16},{16,24},{24,32},{32,40},{40,48},{48,56},{56,64},{64,7... | collective-permute-start | bytes 110600 | tf_op jit(solution)/shard_map/ppermute | solution.py:13
  395.4 24.6 %all-to-all-start.2 = ((bf16[128,32,32]{0,2,1:T(8,128)(2,1)}), bf16[128,32,32]{0,2,1:T(8,128)(2,1)S(1)}, u32[]{:S(2)}, u32[]{:S(2)}) async-start(bf16[128,32,32]{0,2,1:T(8,128)(2,1)} %bitcast.9), calls=%async_computation.3 | async-start | bytes 524288 | tf_op jit(solution)/shard_map/all_to_all | solution.py:138
  404.5 71.5 %reduce-scatter.2.cloned.1.call-start = ((), (), s32[]{:S(2)}) async-start(), calls=%async_computation.8 | async-start | bytes 2359296 | tf_op jit(solution)/shard_map/reduce_scatter | solution.py:122
  417.3 2.7 copy-start.12
  417.3 2.7 copy-start.14
  417.3 2.7 copy-start.16
  417.3 2.6 copy-start.18
  417.5 2.5 copy-start.20
  420.0 24.6 %all-to-all-start.1 = ((bf16[128,32,32]{0,2,1:T(8,128)(2,1)}), bf16[128,32,32]{0,2,1:T(8,128)(2,1)S(1)}, u32[]{:S(2)}, u32[]{:S(2)}) async-start(bf16[128,32,32]{0,2,1:T(8,128)(2,1)} %bitcast.3), calls=%async_computation.2 | async-start | bytes 524288 | tf_op jit(solution)/shard_map/all_to_all | solution.py:142
  477.8 23.9 %all-to-all-start.4 = ((bf16[128,32,32]{0,2,1:T(8,128)(2,1)}), bf16[128,32,32]{0,2,1:T(8,128)(2,1)S(1)}, u32[]{:S(2)}, u32[]{:S(2)}) async-start(bf16[128,32,32]{0,2,1:T(8,128)(2,1)} %bitcast.23), calls=%async_computation.5 | async-start | bytes 524288 | tf_op jit(solution)/shard_map/all_to_all | solution.py:150
  507.4 2.1 copy-start.5
  536.1 5.9 copy-start.6
  536.1 18.7 %all-to-all-start.3 = ((bf16[32,128,32]{1,2,0:T(8,128)(2,1)}), bf16[32,128,32]{1,2,0:T(8,128)(2,1)S(1)}, u32[]{:S(2)}, u32[]{:S(2)}) async-start(bf16[32,128,32]{1,2,0:T(8,128)(2,1)} %copy.52), calls=%async_computation.4 | async-start | bytes 524288 | tf_op jit(solution)/shard_map/all_to_all | solution.py:147
  554.8 18.5 %all-to-all-start.5 = ((bf16[32,128,32]{1,2,0:T(8,128)(2,1)}), bf16[32,128,32]{1,2,0:T(8,128)(2,1)S(1)}, u32[]{:S(2)}, u32[]{:S(2)}) async-start(bf16[32,128,32]{1,2,0:T(8,128)(2,1)} %copy.61), calls=%async_computation.6 | async-start | bytes 524288 | tf_op jit(solution)/shard_map/all_to_all | solution.py:156
  573.3 18.5 %all-to-all-start.6 = ((bf16[32,128,32]{1,2,0:T(8,128)(2,1)}), bf16[32,128,32]{1,2,0:T(8,128)(2,1)S(1)}, u32[]{:S(2)}, u32[]{:S(2)}) async-start(bf16[32,128,32]{1,2,0:T(8,128)(2,1)} %copy.66), calls=%async_computation.7 | async-start | bytes 524288 | tf_op jit(solution)/shard_map/all_to_all | solution.py:157
  577.2 254.4 %all-reduce.2.cloned.1.call-start = ((), (), s32[]{:S(2)}) async-start(), calls=%async_computation.9 | async-start | bytes 229376 | tf_op jit(solution)/shard_map/psum | solution.py:181
  581.0 11.9 %collective-permute-start.1 = (bf16[6,3,1024]{2,0,1:T(8,128)(2,1)S(1)}, bf16[6,3,1024]{2,0,1:T(8,128)(2,1)S(1)}, u32[]{:S(2)}, u32[]{:S(2)}) collective-permute-start(bf16[6,3,1024]{2,0,1:T(8,128)(2,1)S(1)} %slice.122), channel_id=1, source_target_pairs={{8,0},{16,8},{24,16},{32,24},{40,32},{48,40},{56,48},{64,56},{72,6... | collective-permute-start | bytes 110600 | tf_op jit(solution)/shard_map/ppermute | solution.py:13
  582.4 10.5 %copy-start.11 = (f32[7,3,1024]{2,1,0:T(4,128)}, f32[7,3,1024]{2,1,0:T(4,128)S(1)}, u32[]{:S(2)}) copy-start(f32[7,3,1024]{2,1,0:T(4,128)S(1)} %constant_dynamic-update-slice_fusion) | copy-start | bytes 258052
  593.1 240.1 %copy-start.1 = (bf16[128,1024]{1,0:T(8,128)(2,1)S(1)}, bf16[128,1024]{1,0:T(8,128)(2,1)}, u32[]{:S(2)}) copy-start(bf16[128,1024]{1,0:T(8,128)(2,1)} %param.6) | copy-start | bytes 786436
  (10 other events, 12.5 us)
Sparse Core Ops, SparseCore 0:
  417.4 58.5 reduce-scatter.1
  593.1 238.4 all-reduce.1
